TPU v7x, 32 devices: a whole 2x2x4 slice. The times are simulated.
32 devices in a mesh: groups: 2 (over x), seq: 8 (over z, y), head: 2 (over core).
Axes of the slice: x: 2, y: 2, z: 4, core: 2. Of those that a mesh axis runs over, the one named last changes fastest.
Arguments:
- x_input: bfloat16 [2048, 4096], P(('groups', 'seq'), 'head'), parts along dimension 0, may hold values from -6 to 6
- b_rows: bfloat16 [2048, 128], P(('groups', 'seq')), parts along dimension 0, may hold values from -0.5 to 0.5
- c_rows: bfloat16 [2048, 128], P(('groups', 'seq')), parts along dimension 0, may hold values from -0.5 to 0.5
- decay_log: float32 [64, 1024], P(('groups', 'head'), 'seq'), parts along dimension 0, may hold values from -1 to 0
- skip_gain: float32 [32], P('head'), may hold values from 0.5 to 1.5
- doc_lengths: int32 [8], P('groups'), parts along dimension 0, may hold values from 1 to 512, 1024 in all
- queries: bfloat16 [2048, 2048], P(('groups', 'seq'), 'head'), parts along dimension 0, may hold values from -9 to 9
- attention_key_rows: bfloat16 [2048, 512], P(('groups', 'seq'), 'head'), parts along dimension 0, may hold values from -9 to 9
- values: bfloat16 [2048, 512], P(('groups', 'seq'), 'head'), parts along dimension 0, may hold values from -6 to 6
- mixer_cot: bfloat16 [2048, 4096], P(('groups', 'seq'), 'head'), parts along dimension 0, may hold values from -6 to 6
- attention_output_cotangent: bfloat16 [2048, 2048], P(('groups', 'seq'), 'head'), parts along dimension 0, may hold values from -6 to 6
Outputs:
- mixer_out: bfloat16 [2048, 4096], P(('groups', 'seq'), 'head'), parts along dimension 0
- attn_out: bfloat16 [2048, 2048], P(('groups', 'seq'), 'head'), parts along dimension 0
- x_grad: bfloat16 [2048, 4096], P(('groups', 'seq'), 'head'), parts along dimension 0
- b_grad: float32 [2048, 128], P(('groups', 'seq')), parts along dimension 0
- c_grad: float32 [2048, 128], P(('groups', 'seq')), parts along dimension 0
- decay_grad: float32 [64, 1024], P(('groups', 'head'), 'seq'), parts along dimension 0
- q_grad: bfloat16 [2048, 2048], P(('groups', 'seq'), 'head'), parts along dimension 0
- key_gradient: bfloat16 [2048, 512], P(('groups', 'seq'), 'head'), parts along dimension 0
- value_gradient: bfloat16 [2048, 512], P(('groups', 'seq'), 'head'), parts along dimension 0
There are 2 independent parts, one for each index of `groups`. A program takes and returns all parts, laid end to end along the dimension named above; an argument that names none is the same for every part. Nothing has to cross between parts.
Inputs may be any that keep to these rules, and one draw needn't show every extreme that they name: `doc_lengths`: the lengths of the documents packed into the stream, in order; they sum to 1024.
All inputs are finite; a program needn't handle non-finite values.
Results may differ from a plain program's by a relative error of at most 0.023.
Values may be sent and summed in bfloat16 or wider, within the bound.
No kernel may reach another device: no remote copies, remote signals or barrier semaphores. Data moves between devices by JAX's collectives and lax.ppermute only.
A program may use at most 128 MiB of HBM per device.

v0:
```python
import math
import jax
import jax.numpy as jnp
from jax import lax
from jax.sharding import PartitionSpec as P

P_SIZE = 128
HEAD_SIZE = 128
TOK_SPAN = 128
precise = lax.Precision.HIGHEST
big_negative = -1e30


def entering_2(part, axis, combine, identity, reverse):
    count = lax.axis_size(axis)
    place = lax.axis_index(axis)
    ahead = count - 1 - place if reverse else place
    early = jax.tree.map(lambda a, e: jnp.zeros_like(a) + jnp.asarray(e, a.dtype), part, identity)
    span = part
    shift = 1
    while shift < count:
        if reverse:
            pairs = [(i, i - shift) for i in range(shift, count)]
        else:
            pairs = [(i, i + shift) for i in range(count - shift)]
        got = lax.ppermute(span, axis, pairs)
        have = ahead >= shift
        got = jax.tree.map(lambda g, e: jnp.where(have, g, jnp.asarray(e, g.dtype)), got, identity)
        early = combine(got, early)
        if 2 * shift < count:
            span = combine(got, span)
        shift *= 2
    return early


def doc_index(positions, lengths):
    ends = jnp.cumsum(lengths)
    return jnp.sum((positions[:, None] >= ends[None, :]).astype(jnp.int32), axis=1)


def cumulate(decay):
    return jnp.cumsum(decay, axis=1)


def local_state(inputs, b_float, cumulated, segment):
    weights = (
        jnp.exp(cumulated[:, -1:] - cumulated)
        * (segment == segment[-1]).astype(inputs.dtype)[None, :]
    )
    return jnp.einsum("hs,sn,shp->hnp", weights, b_float, inputs, precision=precise)


def carry_factor(cumulated, segment, before):
    return jnp.exp(cumulated[:, -1]) * (segment[-1] == before).astype(cumulated.dtype)


def mixer_stretch(inputs, b_float, c_float, decay, gains, segment, before, state_in):
    cumulated = cumulate(decay)
    width = inputs.shape[0]
    steps = jnp.arange(width)
    allowed = (steps[:, None] >= steps[None, :]) & (segment[:, None] == segment[None, :])
    gaps = jnp.where(allowed[None], cumulated[:, :, None] - cumulated[:, None, :], big_negative)
    kernel = jnp.exp(gaps) * jnp.dot(c_float, b_float.T, precision=precise)[None]
    inner = jnp.einsum("hts,shp->thp", kernel, inputs, precision=precise)
    keeps = (segment == before).astype(inputs.dtype)
    entering = jnp.einsum("tn,hnp->thp", c_float, state_in, precision=precise)
    reach = jnp.exp(cumulated).T * keeps[:, None]
    outputs = inner + reach[:, :, None] * entering + gains[None, :, None] * inputs
    factor = carry_factor(cumulated, segment, before)
    state_out = factor[:, None, None] * state_in + local_state(inputs, b_float, cumulated, segment)
    return (outputs, state_out)


def combine_states(earlier, later):
    return (earlier[0] * later[0], later[0][:, None, None] * earlier[1] + later[1])


def mixer_whole(inputs, b_float, c_float, decay, gains, segment):
    width = TOK_SPAN
    count = inputs.shape[0] // width
    heads = inputs.shape[1]
    inp = inputs.reshape(count, width, heads, P_SIZE)
    b_blocks = b_float.reshape(count, width, -1)
    c_blocks = c_float.reshape(count, width, -1)
    dec = decay.reshape(heads, count, width).transpose(1, 0, 2)
    seg = segment.reshape(count, width)
    befores = jnp.concatenate([jnp.full((1,), -1, seg.dtype), seg[:-1, -1]])
    cumulated = jnp.cumsum(dec, axis=2)
    factor = jax.vmap(carry_factor)(cumulated, seg, befores)
    summary = jax.vmap(local_state)(inp, b_blocks, cumulated, seg)

    def advance(carried, pieces):
        fac, summ = pieces
        return (fac[:, None, None] * carried + summ, carried)

    unused, state_in = lax.scan(advance, jnp.zeros_like(summary[0]), (factor, summary))

    def stretch(i, brow, crow, d, sg, bf, st):
        return mixer_stretch(i, brow, crow, d, gains, sg, bf, st)[0]

    outputs = jax.vmap(stretch)(inp, b_blocks, c_blocks, dec, seg, befores, state_in)
    return outputs.reshape(count * width, heads, P_SIZE)


def mamba_by_heads(x_input, b_all, c_all, decay_log, skip_gain, doc_lengths, mixer_cot):
    seq_count = lax.axis_size("seq")
    place = lax.axis_index("seq")
    tokens = x_input.shape[0]
    heads_here = skip_gain.shape[0]
    own = heads_here // seq_count
    total = tokens * seq_count
    pair = lax.all_to_all(
        jnp.stack([x_input, mixer_cot]), "seq", split_axis=2, concat_axis=1, tiled=True
    )
    decay = lax.all_to_all(decay_log, "seq", split_axis=0, concat_axis=1, tiled=True)
    gains = lax.dynamic_slice_in_dim(skip_gain, place * own, own)
    segment = doc_index(jnp.arange(total, dtype=jnp.int32), doc_lengths)
    inputs = pair[0].astype(jnp.float32).reshape(total, own, P_SIZE)
    cot = pair[1].astype(jnp.float32).reshape(total, own, P_SIZE)

    def whole_of(i, brow, crow, d):
        return mixer_whole(i, brow, crow, d, gains, segment)

    mixed, pull = jax.vjp(
        whole_of, inputs, b_all.astype(jnp.float32), c_all.astype(jnp.float32), decay
    )
    grad_x, grad_b, grad_c, grad_decay = pull(cot)
    back = jnp.stack(
        [
            mixed.reshape(total, own * P_SIZE).astype(jnp.bfloat16),
            grad_x.reshape(total, own * P_SIZE).astype(jnp.bfloat16),
        ]
    )
    back = lax.all_to_all(back, "seq", split_axis=1, concat_axis=2, tiled=True)
    grad_decay = lax.all_to_all(grad_decay, "seq", split_axis=1, concat_axis=0, tiled=True)
    return (back[0], back[1], jnp.concatenate([grad_b, grad_c], axis=1), grad_decay)


def mamba_by_stretch(
    x_input, b_rows, c_rows, decay_log, skip_gain, doc_lengths, mixer_cot, segment, offset
):
    tokens = x_input.shape[0]
    previous = doc_index(jnp.reshape(offset - 1, (1,)), doc_lengths)[0]
    before = jnp.where(offset > 0, previous, -1)
    heads_here = skip_gain.shape[0]
    inputs = x_input.astype(jnp.float32).reshape(tokens, heads_here, P_SIZE)
    b_float = b_rows.astype(jnp.float32)
    c_float = c_rows.astype(jnp.float32)
    cot_float = mixer_cot.astype(jnp.float32).reshape(tokens, heads_here, P_SIZE)

    def stretch_of(inp, brow, crow, decay, state_in):
        return mixer_stretch(inp, brow, crow, decay, skip_gain, segment, before, state_in)

    cumulated = cumulate(decay_log)
    factor = carry_factor(cumulated, segment, before)
    summary = local_state(inputs, b_float, cumulated, segment)
    zero_state = jnp.zeros_like(summary)
    identity = (jnp.ones_like(factor), zero_state)
    state_in = entering_2((factor, summary), "seq", combine_states, identity, False)[1]
    (mixed, state_out), pull = jax.vjp(stretch_of, inputs, b_float, c_float, decay_log, state_in)
    adjoint_local = pull((cot_float, zero_state))[4]
    adjoint_out = entering_2((factor, adjoint_local), "seq", combine_states, identity, True)[1]
    grad_x, grad_b, grad_c, grad_decay, unused = pull((cot_float, adjoint_out))
    head_count = lax.axis_size("head")
    if head_count == 2:
        other_b, other_c = lax.ppermute((grad_b, grad_c), "head", [(0, 1), (1, 0)])
        grad_b, grad_c = (grad_b + other_b, grad_c + other_c)
    else:
        grad_b, grad_c = lax.psum((grad_b, grad_c), "head")
    mixer_out = mixed.reshape(tokens, heads_here * P_SIZE).astype(jnp.bfloat16)
    x_grad = grad_x.reshape(tokens, heads_here * P_SIZE).astype(jnp.bfloat16)
    return (mixer_out, x_grad, grad_b, grad_c, grad_decay)


def on_device(
    x_input,
    b_rows,
    c_rows,
    decay_log,
    skip_gain,
    doc_lengths,
    queries,
    attention_key_rows,
    values,
    mixer_cot,
    attention_output_cotangent,
):
    tokens = x_input.shape[0]
    offset = lax.axis_index("seq") * tokens
    total_len = tokens * lax.axis_size("seq")
    positions = offset + jnp.arange(tokens, dtype=jnp.int32)
    segment = doc_index(positions, doc_lengths)
    heads_here = skip_gain.shape[0]
    by_heads = heads_here % lax.axis_size("seq") == 0
    key_width = attention_key_rows.shape[1]
    state_width = b_rows.shape[1]
    pieces = [attention_key_rows, values] + ([b_rows, c_rows] if by_heads else [])
    gathered = lax.all_gather(jnp.concatenate(pieces, axis=1), "seq", axis=0, tiled=True)
    key_all, value_all = (gathered[:, :key_width], gathered[:, key_width : 2 * key_width])
    if by_heads:
        b_all = gathered[:, 2 * key_width : 2 * key_width + state_width]
        c_all = gathered[:, 2 * key_width + state_width :]
        mixer_out, x_grad, bc_part, grad_decay = mamba_by_heads(
            x_input, b_all, c_all, decay_log, skip_gain, doc_lengths, mixer_cot
        )
    else:
        mixer_out, x_grad, grad_b, grad_c, grad_decay = mamba_by_stretch(
            x_input, b_rows, c_rows, decay_log, skip_gain, doc_lengths, mixer_cot, segment, offset
        )
    logit_scale = 1.0 / math.sqrt(HEAD_SIZE)
    groups = attention_key_rows.shape[1] // HEAD_SIZE
    heads_per_group = queries.shape[1] // HEAD_SIZE // groups
    key_span = min(512, total_len)
    blocks = total_len // key_span
    last_pos = offset + tokens - 1
    query_grid = queries.reshape(tokens, groups, heads_per_group, HEAD_SIZE)
    cotangent_table = attention_output_cotangent.reshape(tokens, groups, heads_per_group, HEAD_SIZE)

    def block_view(number):
        anchor = number * key_span
        key_blk = lax.dynamic_slice_in_dim(key_all, anchor, key_span, 0).reshape(
            key_span, groups, HEAD_SIZE
        )
        value_blk = lax.dynamic_slice_in_dim(value_all, anchor, key_span, 0).reshape(
            key_span, groups, HEAD_SIZE
        )
        key_pos = anchor + jnp.arange(key_span, dtype=jnp.int32)
        allowed = (key_pos[None, :] <= positions[:, None]) & (
            doc_index(key_pos, doc_lengths)[None, :] == segment[:, None]
        )
        scores = (
            jnp.einsum("tgrd,kgd->grtk", query_grid, key_blk, preferred_element_type=jnp.float32)
            * logit_scale
        )
        scores = jnp.where(allowed[None, None], scores, big_negative)
        return (anchor, key_blk, value_blk, allowed, scores)

    def visit(number, carried, work):
        return lax.cond(
            number * key_span <= last_pos,
            lambda inner: work(number, inner),
            lambda inner: inner,
            carried,
        )

    def stats_step(number, carried):
        row_peak, row_total = carried
        anchor, key_blk, value_blk, allowed, scores = block_view(number)
        new_peak = jnp.maximum(row_peak, jnp.max(scores, axis=-1))
        fresh = jnp.sum(
            jnp.where(allowed[None, None], jnp.exp(scores - new_peak[..., None]), 0.0), axis=-1
        )
        return (new_peak, row_total * jnp.exp(row_peak - new_peak) + fresh)

    stat_shape = (groups, heads_per_group, tokens)
    row_peak, row_total = lax.fori_loop(
        0,
        blocks,
        lambda number, carried: visit(number, carried, stats_step),
        (jnp.full(stat_shape, big_negative, jnp.float32), jnp.zeros(stat_shape, jnp.float32)),
    )
    log_norm = row_peak + jnp.log(row_total)

    def output_step(number, totals):
        anchor, key_blk, value_blk, allowed, scores = block_view(number)
        weights = jnp.where(allowed[None, None], jnp.exp(scores - log_norm[..., None]), 0.0).astype(
            jnp.bfloat16
        )
        return totals + jnp.einsum(
            "grtk,kgd->tgrd", weights, value_blk, preferred_element_type=jnp.float32
        )

    attention_table = lax.fori_loop(
        0,
        blocks,
        lambda number, carried: visit(number, carried, output_step),
        jnp.zeros((tokens, groups, heads_per_group, HEAD_SIZE), jnp.float32),
    ).astype(jnp.bfloat16)
    row_products = jnp.einsum(
        "bkfh,bkfh->kfb", cotangent_table, attention_table, preferred_element_type=jnp.float32
    )

    def grad_terms(allowed, scores, value_blk):
        probs_full = jnp.where(allowed[None, None], jnp.exp(scores - log_norm[..., None]), 0.0)
        grad_prob = jnp.einsum(
            "tgrd,kgd->grtk", cotangent_table, value_blk, preferred_element_type=jnp.float32
        )
        grad_score = (probs_full * (grad_prob - row_products[..., None])).astype(jnp.bfloat16)
        return (probs_full.astype(jnp.bfloat16), grad_score)

    query_zero = jnp.zeros((tokens, groups, heads_per_group, HEAD_SIZE), jnp.float32)

    def full_step(number, carried):
        grad_query, term_key, term_value = carried
        anchor, key_blk, value_blk, allowed, scores = block_view(number)
        weights, grad_score = grad_terms(allowed, scores, value_blk)
        grad_query = grad_query + jnp.einsum(
            "grtk,kgd->tgrd", grad_score, key_blk, preferred_element_type=jnp.float32
        )
        key_part = jnp.einsum(
            "grtk,tgrd->kgd", grad_score, query_grid, preferred_element_type=jnp.float32
        ).reshape(key_span, groups * HEAD_SIZE)
        value_part = jnp.einsum(
            "grtk,tgrd->kgd", weights, cotangent_table, preferred_element_type=jnp.float32
        ).reshape(key_span, groups * HEAD_SIZE)
        term_key = lax.dynamic_update_slice_in_dim(term_key, key_part, anchor, 0)
        term_value = lax.dynamic_update_slice_in_dim(term_value, value_part, anchor, 0)
        return (grad_query, term_key, term_value)

    term_zero = jnp.zeros((total_len, groups * HEAD_SIZE), jnp.float32)
    grad_query, term_key, term_value = lax.fori_loop(
        0,
        blocks,
        lambda number, carried: visit(number, carried, full_step),
        (query_zero, term_zero, term_zero),
    )
    sums = [term_key, term_value] + ([bc_part] if by_heads else [])
    kv_total = lax.psum_scatter(
        jnp.concatenate(sums, axis=1), "seq", scatter_dimension=0, tiled=True
    )
    key_gradient_total = kv_total[:, : groups * HEAD_SIZE]
    value_gradient_total = kv_total[:, groups * HEAD_SIZE : 2 * groups * HEAD_SIZE]
    if by_heads:
        bc_sum = kv_total[:, 2 * groups * HEAD_SIZE :]
        if lax.axis_size("head") == 2:
            bc_sum = bc_sum + lax.ppermute(bc_sum, "head", [(0, 1), (1, 0)])
        else:
            bc_sum = lax.psum(bc_sum, "head")
        grad_b, grad_c = (bc_sum[:, :state_width], bc_sum[:, state_width:])
    attn_out = attention_table.reshape(tokens, groups * heads_per_group * HEAD_SIZE)
    q_grad = (
        (grad_query * logit_scale)
        .reshape(tokens, groups * heads_per_group * HEAD_SIZE)
        .astype(jnp.bfloat16)
    )
    key_gradient = (key_gradient_total * logit_scale).astype(jnp.bfloat16)
    value_gradient = value_gradient_total.astype(jnp.bfloat16)
    return (
        mixer_out,
        attn_out,
        x_grad,
        grad_b,
        grad_c,
        grad_decay,
        q_grad,
        key_gradient,
        value_gradient,
    )


def solution(mesh):
    placed = (
        P(("groups", "seq"), "head"),
        P(("groups", "seq"), None),
        P(("groups", "seq"), None),
        P(("groups", "head"), "seq"),
        P("head"),
        P("groups"),
        P(("groups", "seq"), "head"),
        P(("groups", "seq"), "head"),
        P(("groups", "seq"), "head"),
        P(("groups", "seq"), "head"),
        P(("groups", "seq"), "head"),
    )
    return jax.shard_map(
        on_device,
        mesh=mesh,
        in_specs=placed,
        out_specs=(
            P(("groups", "seq"), "head"),
            P(("groups", "seq"), "head"),
            P(("groups", "seq"), "head"),
            P(("groups", "seq"), None),
            P(("groups", "seq"), None),
            P(("groups", "head"), "seq"),
            P(("groups", "seq"), "head"),
            P(("groups", "seq"), "head"),
            P(("groups", "seq"), "head"),
        ),
        check_vma=False,
    )
```

profile of v0, /device:TPU:1, one launch (start us, length us, event | category | flops | bytes accessed | tf_op | source)
XLA Modules:
  0.0 266.9 jit_solution(8798041764163728764)
XLA Ops:
  11.6 6.4 %all-to-all-start.1 = ((f32[8,2,128]{2,1,0:T(2,128)}), f32[8,2,128]{2,1,0:T(2,128)S(1)}, u32[]{:S(2)}, u32[]{:S(2)}) async-start(f32[8,2,128]{2,1,0:T(2,128)} %bitcast.332), calls=%async_computation.1 | async-start | bytes 16384 | tf_op jit(solution)/shard_map/all_to_all | solution.py:115
  18.8 1.3 pad_maximum_fusion.1
  20.2 2.0 copy.341
  23.4 4.3 %all-to-all-start = ((bf16[2,128,2048]{1,0,2:T(2,128)(2,1)}), bf16[2,128,2048]{1,0,2:T(2,128)(2,1)S(1)}, u32[]{:S(2)}, u32[]{:S(2)}) async-start(bf16[2,128,2048]{1,0,2:T(2,128)(2,1)} %copy.341), calls=%async_computation | async-start | bytes 2097152 | tf_op jit(solution)/shard_map/all_to_all | solution.py:112
  33.2 34.0 %all-to-all-done = bf16[2,128,2048]{1,0,2:T(2,128)(2,1)S(1)} async-done(((bf16[2,128,2048]{1,0,2:T(2,128)(2,1)}), bf16[2,128,2048]{1,0,2:T(2,128)(2,1)S(1)}, u32[]{:S(2)}, u32[]{:S(2)}) %all-to-all-start) | async-done | bytes 1048608 | tf_op jit(solution)/shard_map/all_to_all | solution.py:112
  67.5 2.4 all-gather.2.cloned.1.call-done
  72.5 2.3 fusion.35
  74.9 23.3 %while.88 = (s32[]{:T(128)}, f32[2,128,128]{2,1,0:T(8,128)S(1)}, f32[8,2,128,128]{3,2,1,0:T(8,128)S(1)}, f32[8,2,1,1]{1,3,2,0:T(1,128)}, f32[8,2]{1,0:T(8,128)},...) while((s32[]{:T(128)}, f32[2,128,128]{2,1,0:T(8,128)S(1)}, ...), condition=%wide.region_4.5_spmd.clone, body=%wide.region_3.4_spmd.clone.sunk | while | flops 131075 | bytes 656528 | solution.py:96
  76.6 1.2 constant_dynamic-update-slice_fusion.4
  79.5 1.2 constant_dynamic-update-slice_fusion.4
  82.4 1.2 constant_dynamic-update-slice_fusion.4
  85.3 1.2 constant_dynamic-update-slice_fusion.4
  88.2 1.2 constant_dynamic-update-slice_fusion.4
  91.2 1.2 constant_dynamic-update-slice_fusion.4
  98.2 1.3 copy.357
  99.5 2.9 %fusion.52 = (f32[8,128,2]{1,2,0:T(2,128)S(1)}, f32[8,128,256]{1,2,0}) fusion(bf16[8,128,2,128]{1,3,2,0:T(8,128)(2,1)S(1)} %bitcast.283, bf16[8,128,128]{2,1,0:T(8,128)(2,1)S(1)} %bitcast.294, f32[8,128,256]{1,2,0:T(8,128)} %bitcast.306), kind=kOutput, calls=%fused_computation.87 | convolution fusion | flops 403437568 | bytes 2891776
  102.5 1.5 fusion.59
  104.0 2.7 %fusion.51 = f32[8,128,128]{2,1,0:T(8,128)} fusion(f32[8,2,128,128]{3,2,1,0:T(8,128)S(1)} %get-tuple-element.1737, bf16[8,128,2,128]{1,3,2,0:T(8,128)(2,1)S(1)} %bitcast.285, f32[8,128,2]{1,2,0:T(2,128)S(1)} %copy.352), kind=kOutput, calls=%fused_computation.84 | convolution fusion | flops 403177472 | bytes 2105344 | tf_op jit(solution)/shard_map/transpose(jvp(vmap(tn,hnp->thp)))/dot_general | solution.py:66
  106.8 1.6 convolution_bitcast_fusion.1
  108.5 14.9 %while.89 = (s32[]{:T(128)}, f32[2,128,128]{2,1,0:T(8,128)S(1)}, f32[8,2]{1,0:T(8,128)S(1)}, f32[8,2,128,128]{3,2,1,0:T(8,128)S(1)}, f32[8,2,128,128]{2,3,1,0:T(...) while((s32[]{:T(128)}, f32[2,128,128]{2,1,0:T(8,128)S(1)}, ...), condition=%wide.region_7.8_spmd.clone, body=%wide.region_5.7_spmd.clone.sunk | while | flops 196610 | bytes 1310920 | solution.py:96
  123.5 1.3 fusion.83
  124.8 1.8 while.85
  124.8 1.7 conditional.9
  127.4 3.3 %while.86 = (s32[]{:T(128)}, f32[128,2,4,128]{0,3,2,1:T(8,128)}, s32[]{:T(128)}, bf16[1024,256]{0,1:T(8,128)(2,1)S(1)}, s32[4]{0:T(128)S(1)}, /*index=5*/s32[128...) while((s32[]{:T(128)}, f32[128,2,4,128]{0,3,2,1:T(8,128)}, ...), condition=%wide.region_22.23_spmd.clone, body=%wide.region_17.22_spmd.clone.sunk | while | flops 271390848 | bytes 3031901 | solution.py:273
  127.4 3.3 %conditional.10 = (f32[128,2,4,128]{0,3,2,1:T(8,128)}) conditional(s32[]{:T(128)} %convert_element_type.165, f32[128,2,4,128]{0,3,2,1:T(8,128)} %get-tuple-element.1807, (s32[]{:T(128)}, bf16[1024,256]{0,1:T(8,128)(2,1)S(1)}, s32[]{:T(128)}, s32[4]{0:T(128)S(1)}, s32[128]{0:T(128)S(1)}, /*index=5*/bf16[1024,256]{0,1:T(8,128)(2,1)S(1)}, ...), branch_computations={%region_18.18_spmd, %region_19.21_spmd} | conditional | flops 271390848 | bytes 3031158 | solution.py:239
  128.0 2.8 %fusion.13 = f32[128,2,4,128]{0,3,2,1:T(8,128)} fusion(f32[128,2,4,128]{0,3,2,1:T(8,128)} %get-tuple-element.792, bf16[512,2,128,1]{0,2,3,1:T(8,128)(2,1)S(1)} %bitcast.298, bf16[512,2,128,1]{0,2,3,1:T(8,128)(2,1)S(1)} %bitcast.297, bf16[128,2,4,128]{3,0,2,1:T(8,128)(2,1)S(1)} %get-tuple-element.799, f32[2,4,128]{2,1,0:T(4,128)S(1)} %get-tuple-element.800, ...), kind=kOutput, calls=%fused_computation.19 | convolution fusion | flops 271187968 | bytes 1904640 | tf_op jit(solution)/shard_map/while/body/eval_jaxpr/cond/branch_1_fun/grtk,kgd->tgrd/dot_general | solution.py:269
  130.7 3.5 %fusion.53 = (f32[8,128,128]{1,2,0:T(8,128)}, f32[8,2,128,128]{3,2,1,0:T(8,128)}) fusion(f32[8,128,2]{1,2,0:T(2,128)S(1)} %copy.353, f32[8,2,128,128]{3,2,1,0:T(8,128)S(1)} %get-tuple-element.864, bf16[8,128,2,128]{1,3,2,0:T(8,128)(2,1)} %bitcast.301), kind=kOutput, calls=%fused_computation.91 | convolution fusion | flops 403046400 | bytes 3153920 | tf_op jit(solution)/shard_map/transpose(jvp(vmap(hs,sn,shp->hnp)))/dot_general | solution.py:50
  134.3 2.1 copy.423
  136.4 2.5 convolution_add_fusion
  138.9 1.5 convolution_add_fusion.1
  140.4 1.8 fusion.60
  144.5 5.8 %while.87 = (s32[]{:T(128)}, f32[128,2,4,128]{0,3,2,1:T(8,128)S(1)}, f32[1024,256]{0,1:T(8,128)}, f32[1024,256]{0,1:T(8,128)}, s32[]{:T(128)}, /*index=5*/bf16[1...) while((s32[]{:T(128)}, ...), condition=%wide.region_28.29_spmd.clone, body=%wide.region_23.28_spmd.clone.sunk | while | flops 675616896 | bytes 33444932 | solution.py:311
  144.5 5.8 %conditional.11 = ((f32[128,2,4,128]{0,3,2,1:T(8,128)S(1)}, f32[1024,256]{0,1:T(8,128)}, f32[1024,256]{0,1:T(8,128)})) conditional(s32[]{:T(128)} %convert_element_type.166, (f32[128,2,4,128]{0,3,2,1:T(8,128)S(1)}, f32[1024,256]{0,1:T(8,128)}, f32[1024,256]{0,1:T(8,128)}) %tuple.226, (s32[]{:T(128)}, bf16[1024,256]{0,1:T(8,128)(2,1)S(1)}, ...), branch_computations={%region_24.24_spmd, %region_25.27_spmd} | conditional | flops 675616896 | bytes 33444102 | solution.py:239
  150.3 2.7 %copy.377 = f32[1024,256]{1,0:T(8,128)} copy(f32[1024,256]{0,1:T(8,128)} %get-tuple-element.869) | data formatting | bytes 2097152 | tf_op jit(solution)/shard_map/while | solution.py:311
  152.9 1.3 copy.376
  154.3 3.6 %pad_maximum_fusion = f32[1024,768]{1,0:T(8,128)} fusion(f32[1024,128]{1,0:T(8,128)S(1)} %bitcast.307, f32[1024,128]{1,0:T(8,128)} %bitcast.308, f32[1024,256]{1,0:T(8,128)} %copy.377, f32[1024,256]{1,0:T(8,128)} %copy.376), kind=kLoop, calls=%fused_computation.65 | loop fusion | flops 2359296 | bytes 6291456 | tf_op jit(solution)/shard_map/concatenate | solution.py:319
  159.8 2.1 fusion.43
  161.9 2.3 fusion.47
  164.9 3.0 %fusion.46 = bf16[8,128,2,128]{1,3,2,0:T(8,128)(2,1)S(1)} fusion(bf16[8,128,2,128]{1,3,2,0:T(8,128)(2,1)S(1)} %bitcast.302, f32[8,128,2,128]{1,3,2,0:T(8,128)} %bitcast.314, f32[2]{0:T(128)S(1)} %dynamic_slice.54, f32[8,128,2]{1,2,0:T(2,128)S(1)} %copy.352, f32[8,128,128]{2,1,0:T(8,128)} %fusion.90, f32[8,2,128]{2,1,0:T(2,128)S(1)} %copy-done.36, ...), kind=kOutput, calls=%fused_computation.81 | convolution fusion | flops 405012480 | bytes 2768904 | tf_op jit(solution)/shard_map/jvp(vmap(hts,shp->thp))/dot_general | solution.py:64
  169.8 2.5 reduce_window_sum.46
  172.4 2.5 reduce_window_sum.47
  175.5 13.2 %all-to-all-start.3 = ((f32[2,8,128]{2,0,1:T(2,128)}), f32[2,8,128]{2,0,1:T(2,128)S(1)}, u32[]{:S(2)}, u32[]{:S(2)}) async-start(f32[2,8,128]{2,0,1:T(2,128)} %copy.384), calls=%async_computation.4 | async-start | bytes 16384 | tf_op jit(solution)/shard_map/all_to_all | solution.py:135
  188.8 2.1 copy.362
  190.9 3.4 %all-to-all-done.3 = f32[2,8,128]{2,0,1:T(2,128)S(1)} async-done(((f32[2,8,128]{2,0,1:T(2,128)}), f32[2,8,128]{2,0,1:T(2,128)S(1)}, u32[]{:S(2)}, u32[]{:S(2)}) %all-to-all-start.3) | async-done | bytes 8224 | tf_op jit(solution)/shard_map/all_to_all | solution.py:135
  194.3 3.6 %all-to-all-start.2 = ((bf16[2,1024,256]{2,0,1:T(2,128)(2,1)}), bf16[2,1024,256]{2,0,1:T(2,128)(2,1)S(1)}, u32[]{:S(2)}, u32[]{:S(2)}) async-start(bf16[2,1024,256]{2,0,1:T(2,128)(2,1)} %copy.362), calls=%async_computation.2 | async-start | bytes 2097152 | tf_op jit(solution)/shard_map/all_to_all | solution.py:134
  199.7 25.4 %all-to-all-done.2 = bf16[2,1024,256]{2,0,1:T(2,128)(2,1)S(1)} async-done(((bf16[2,1024,256]{2,0,1:T(2,128)(2,1)}), bf16[2,1024,256]{2,0,1:T(2,128)(2,1)S(1)}, u32[]{:S(2)}, u32[]{:S(2)}) %all-to-all-start.2) | async-done | bytes 1048608 | tf_op jit(solution)/shard_map/all_to_all | solution.py:134
  225.2 27.3 %reduce-scatter.2.cloned.1.call-done = f32[128,768]{1,0:T(8,128)} async-done(((f32[1024,768]{1,0:T(8,128)}), f32[128,768]{1,0:T(8,128)}) %reduce-scatter.2.cloned.1.call-update) | async-done | bytes 393232 | tf_op jit(solution)/shard_map/reduce_scatter | solution.py:318
  253.4 1.4 collective-permute-start
  (280 shorter events, 69.8 us)
Async XLA Ops:
  7.2 62.7 %all-gather.2.cloned.1.call-start = ((), (), s32[]{:S(2)}) async-start(), calls=%async_computation.5 | async-start | bytes 1769472 | tf_op jit(solution)/shard_map/all_gather | solution.py:198
  11.6 11.8 %all-to-all-start.1 = ((f32[8,2,128]{2,1,0:T(2,128)}), f32[8,2,128]{2,1,0:T(2,128)S(1)}, u32[]{:S(2)}, u32[]{:S(2)}) async-start(f32[8,2,128]{2,1,0:T(2,128)} %bitcast.332), calls=%async_computation.1 | async-start | bytes 16384 | tf_op jit(solution)/shard_map/all_to_all | solution.py:115
  20.2 7.6 %copy-start.26 = (bf16[128,1024]{1,0:T(8,128)(2,1)S(1)}, bf16[128,1024]{1,0:T(8,128)(2,1)}, u32[]{:S(2)}) copy-start(bf16[128,1024]{1,0:T(8,128)(2,1)} %param.37) | copy-start | bytes 786436
  20.2 7.7 %copy-start.27 = (bf16[128,1024]{1,0:T(8,128)(2,1)S(1)}, bf16[128,1024]{1,0:T(8,128)(2,1)}, u32[]{:S(2)}) copy-start(bf16[128,1024]{1,0:T(8,128)(2,1)} %param.33) | copy-start | bytes 786436
  23.4 43.8 %all-to-all-start = ((bf16[2,128,2048]{1,0,2:T(2,128)(2,1)}), bf16[2,128,2048]{1,0,2:T(2,128)(2,1)S(1)}, u32[]{:S(2)}, u32[]{:S(2)}) async-start(bf16[2,128,2048]{1,0,2:T(2,128)(2,1)} %copy.341), calls=%async_computation | async-start | bytes 2097152 | tf_op jit(solution)/shard_map/all_to_all | solution.py:112
  27.7 224.8 %reduce-scatter.2.cloned.1.call-start = ((), (), s32[]{:S(2)}) async-start(), calls=%async_computation.6 | async-start | bytes 3538944 | tf_op jit(solution)/shard_map/reduce_scatter | solution.py:318
  29.6 37.8 %copy-start.37 = (f32[8]{0:T(128)}, f32[8]{0:T(128)S(1)}, u32[]{:S(2)}) copy-start(f32[8]{0:T(128)S(1)} %convert_reduce_fusion.4) | copy-start | bytes 100
  30.9 36.5 %copy-start.31 = (f32[8,128]{1,0:T(8,128)}, f32[8,128]{1,0:T(8,128)S(1)}, u32[]{:S(2)}) copy-start(f32[8,128]{1,0:T(8,128)S(1)} %get-tuple-element.1394) | copy-start | bytes 12292
  31.1 71.3 %copy-start.28 = (pred[8,128,128]{2,1,0:T(8,128)(4,1)}, pred[8,128,128]{2,1,0:T(8,128)(4,1)S(1)}, u32[]{:S(2)}) copy-start(pred[8,128,128]{2,1,0:T(8,128)(4,1)S(1)} %compare_and_fusion.3) | copy-start | bytes 393220
  32.5 35.0 %copy-start.34 = (f32[8,2]{0,1:T(2,128)}, f32[8,2]{0,1:T(2,128)S(1)}, u32[]{:S(2)}) copy-start(f32[8,2]{0,1:T(2,128)S(1)} %slice_reduce_fusion) | copy-start | bytes 196
  67.5 34.9 %copy-start.10 = (bf16[1,8,128,256]{2,3,1,0:T(8,128)(2,1)}, bf16[1,8,128,256]{2,3,1,0:T(8,128)(2,1)S(1)}, u32[]{:S(2)}) copy-start(bf16[1,8,128,256]{2,3,1,0:T(8,128)(2,1)S(1)} %get-tuple-element.1386) | copy-start | bytes 1572868
  67.5 39.2 %copy-start.1 = (bf16[1,8,128,256]{2,3,1,0:T(8,128)(2,1)}, bf16[1,8,128,256]{2,3,1,0:T(8,128)(2,1)S(1)}, u32[]{:S(2)}) copy-start(bf16[1,8,128,256]{2,3,1,0:T(8,128)(2,1)S(1)} %get-tuple-element.1387) | copy-start | bytes 1572868
  71.2 35.6 %copy-start.6 = (bf16[1024,128]{1,0:T(8,128)(2,1)}, bf16[1024,128]{1,0:T(8,128)(2,1)S(1)}, u32[]{:S(2)}) copy-start(bf16[1024,128]{1,0:T(8,128)(2,1)S(1)} %copy.350) | copy-start | bytes 786436
  71.3 3.5 %copy-start.3 = (bf16[1024,128]{1,0:T(8,128)(2,1)}, bf16[1024,128]{1,0:T(8,128)(2,1)S(1)}, u32[]{:S(2)}) copy-start(bf16[1024,128]{1,0:T(8,128)(2,1)S(1)} %copy.351) | copy-start | bytes 786436
  71.4 1.1 copy-start.8
  98.2 4.3 %copy-start.36 = (f32[8,2,128]{2,1,0:T(2,128)S(1)}, f32[8,2,128]{2,1,0:T(2,128)}, u32[]{:S(2)}) copy-start(f32[8,2,128]{2,1,0:T(2,128)} %copy.344) | copy-start | bytes 24580
  99.5 3.0 %copy-start.25 = (f32[8,128,128]{2,1,0:T(8,128)S(1)}, f32[8,128,128]{2,1,0:T(8,128)}, u32[]{:S(2)}) copy-start(f32[8,128,128]{2,1,0:T(8,128)} %fusion.90) | copy-start | bytes 1572868
  102.4 1.6 copy-start.33
  123.4 1.4 copy-start
  123.4 1.4 copy-start.30
  123.4 1.4 copy-start.39
  130.7 5.6 %copy-start.4 = (bf16[1024,128]{1,0:T(8,128)(2,1)S(1)}, bf16[1024,128]{1,0:T(8,128)(2,1)}, u32[]{:S(2)}) copy-start(bf16[1024,128]{1,0:T(8,128)(2,1)} %copy-done.3) | copy-start | bytes 786436
  134.3 4.6 %copy-start.7 = (bf16[1024,128]{1,0:T(8,128)(2,1)S(1)}, bf16[1024,128]{1,0:T(8,128)(2,1)}, u32[]{:S(2)}) copy-start(bf16[1024,128]{1,0:T(8,128)(2,1)} %copy-done.6) | copy-start | bytes 786436
  136.4 2.5 copy-start.18
  136.4 2.5 copy-start.21
  146.6 1.2 copy-start.13
  146.6 1.5 copy-start.16
  148.2 1.0 copy-start.14
  149.2 1.0 copy-start.17
  150.2 2.7 %copy-start.15 = (f32[1024,256]{0,1:T(8,128)S(1)}, f32[1024,256]{0,1:T(8,128)}, u32[]{:S(2)}) copy-start(f32[1024,256]{0,1:T(8,128)} %get-tuple-element.868) | copy-start | bytes 3145732
  150.2 4.0 %copy-start.19 = (f32[8,128,128]{2,1,0:T(8,128)S(1)}, f32[8,128,128]{2,1,0:T(8,128)}, u32[]{:S(2)}) copy-start(f32[8,128,128]{2,1,0:T(8,128)} %convolution_add_fusion) | copy-start | bytes 1572868
  157.9 0.7 copy-start.40
  157.9 1.0 copy-start.5
  157.9 1.9 copy-start.2
  157.9 1.9 copy-start.29
  157.9 4.0 %copy-start.9 = (f32[8,128,128]{2,1,0:T(8,128)S(1)}, f32[8,128,128]{2,1,0:T(8,128)}, u32[]{:S(2)}) copy-start(f32[8,128,128]{2,1,0:T(8,128)} %copy-done.8) | copy-start | bytes 1572868
  161.9 2.9 %copy-start.11 = (bf16[1,8,128,256]{2,3,1,0:T(8,128)(2,1)S(1)}, bf16[1,8,128,256]{2,3,1,0:T(8,128)(2,1)}, u32[]{:S(2)}) copy-start(bf16[1,8,128,256]{2,3,1,0:T(8,128)(2,1)} %copy-done.10) | copy-start | bytes 1572868
  164.8 4.5 %copy-start.35 = (f32[8,2]{0,1:T(2,128)S(1)}, f32[8,2]{0,1:T(2,128)}, u32[]{:S(2)}) copy-start(f32[8,2]{0,1:T(2,128)} %copy-done.34) | copy-start | bytes 196
  164.8 4.5 %copy-start.38 = (f32[8]{0:T(128)S(1)}, f32[8]{0:T(128)}, u32[]{:S(2)}) copy-start(f32[8]{0:T(128)} %copy-done.37) | copy-start | bytes 100
  164.9 4.6 %copy-start.12 = (f32[8,2,128,128]{3,2,1,0:T(8,128)S(1)}, f32[8,2,128,128]{3,2,1,0:T(8,128)}, u32[]{:S(2)}) copy-start(f32[8,2,128,128]{3,2,1,0:T(8,128)} %get-tuple-element.1401) | copy-start | bytes 3145732
  164.9 4.6 %copy-start.20 = (f32[8,128,128]{1,2,0:T(8,128)S(1)}, f32[8,128,128]{1,2,0:T(8,128)}, u32[]{:S(2)}) copy-start(f32[8,128,128]{1,2,0:T(8,128)} %copy.446) | copy-start | bytes 1572868
  167.9 1.7 copy-start.32
  169.2 19.5 %copy-start.22 = (bf16[1,1024,256]{1,2,0:T(8,128)(2,1)S(1)}, bf16[1,1024,256]{1,2,0:T(8,128)(2,1)}, u32[]{:S(2)}) copy-start(bf16[1,1024,256]{1,2,0:T(8,128)(2,1)} %convert_element_type.115) | copy-start | bytes 1572868
  175.5 18.8 %all-to-all-start.3 = ((f32[2,8,128]{2,0,1:T(2,128)}), f32[2,8,128]{2,0,1:T(2,128)S(1)}, u32[]{:S(2)}, u32[]{:S(2)}) async-start(f32[2,8,128]{2,0,1:T(2,128)} %copy.384), calls=%async_computation.4 | async-start | bytes 16384 | tf_op jit(solution)/shard_map/all_to_all | solution.py:135
  188.8 9.1 %copy-start.23 = (bf16[128,2,4,128]{0,3,2,1:T(8,128)(2,1)S(1)}, bf16[128,2,4,128]{0,3,2,1:T(8,128)(2,1)}, u32[]{:S(2)}) copy-start(bf16[128,2,4,128]{0,3,2,1:T(8,128)(2,1)} %get-tuple-element.1371) | copy-start | bytes 786436
  194.3 30.7 %all-to-all-start.2 = ((bf16[2,1024,256]{2,0,1:T(2,128)(2,1)}), bf16[2,1024,256]{2,0,1:T(2,128)(2,1)S(1)}, u32[]{:S(2)}, u32[]{:S(2)}) async-start(bf16[2,1024,256]{2,0,1:T(2,128)(2,1)} %copy.362), calls=%async_computation.2 | async-start | bytes 2097152 | tf_op jit(solution)/shard_map/all_to_all | solution.py:134
  253.4 4.7 %collective-permute-start = (f32[128,256]{1,0:T(8,128)S(1)}, f32[128,256]{1,0:T(8,128)S(1)}, u32[]{:S(2)}, u32[]{:S(2)}) collective-permute-start(f32[128,256]{1,0:T(8,128)S(1)} %slice.80), channel_id=1, source_target_pairs={{0,1},{1,0},{2,3},{3,2},{4,5},{5,4},{6,7},{7,6},{8,9},{9,8},{10,11... | collective-permute-start | bytes 393224 | tf_op jit(solution)/shard_map/ppermute | solution.py:326
  254.9 2.6 copy-start.24
Sparse Core Ops, SparseCore 0:
  11.7 58.1 all-gather.1
  158.0 94.3 reduce-scatter.1
where the time goes:
time: 269 us; the launch traced here: 267 us
  waiting for transfers between devices  93.6 us (35%)
  local copies, waits for them, and re-layouts  68.2 us (25%)
  matrix products  32.8 us (12%)
  starting transfers between devices  29 us (11%)
  other arithmetic  28 us (10%)
  between operations  14.7 us (5%)
    all_to_all x1, waiting for transfers between devices, mamba_by_heads(): lax.all_to_all(jnp.stack([x_input, mixer_cot]), 'seq', split_axis=2, conc...  34 us
    reduce_scatter x1, waiting for transfers between devices, on_device(): lax.psum_scatter(jnp.concatenate(sums, axis=1), 'seq', scatter_dimension=...  27.3 us
    all_to_all x1, waiting for transfers between devices, mamba_by_heads(): back = lax.all_to_all(back, 'seq', split_axis=1, concat_axis=2, tiled=True)  25.4 us
    all_to_all x1, starting transfers between devices, mamba_by_heads(): lax.all_to_all(grad_decay, 'seq', split_axis=1, concat_axis=0, tiled=True)  13.2 us
    mul x16, local copies, waits for them, and re-layouts, advance(): return (fac[:, None, None] * carried + summ, carried)  10.9 us
    unnamed x86, local copies, waits for them, and re-layouts  10.1 us
    dynamic_update_slice x16, local copies, waits for them, and re-layouts, mixer_whole(): lax.scan(advance, jnp.zeros_like(summary[0]), (factor, summary))  9.87 us
    dot_general x3, matrix products, local_state(): jnp.einsum('hs,sn,shp->hnp', weights, b_float, inputs, precision=precise)  8.09 us
  transfers between devices with their start and end apart: 7, of which 6 were waited for; matrix products, arithmetic and copies ran while one was open for 13% of the time, Pallas kernels for 0%

commit v1 on v0

--- a/solution.py
+++ b/solution.py
@@ -112,7 +112,10 @@
     pair = lax.all_to_all(
         jnp.stack([x_input, mixer_cot]), "seq", split_axis=2, concat_axis=1, tiled=True
     )
-    decay = lax.all_to_all(decay_log, "seq", split_axis=0, concat_axis=1, tiled=True)
+    decay = jnp.concatenate(
+        lax.all_to_all(jnp.stack(jnp.split(decay_log, lax.axis_size("seq"), axis=0)), "seq", 0, 0),
+        axis=1,
+    )
     gains = lax.dynamic_slice_in_dim(skip_gain, place * own, own)
     segment = doc_index(jnp.arange(total, dtype=jnp.int32), doc_lengths)
     inputs = pair[0].astype(jnp.float32).reshape(total, own, P_SIZE)

time: 269 us -> 272 us (1.011)
  local copies, waits for them, and re-layouts: 68.2 us -> 77.2 us
  waiting for transfers between devices: 93.6 us -> 86.6 us
    unnamed x86 -> x91, local copies, waits for them, and re-layouts: 10.1 us -> 18.8 us
  transfers between devices with their start and end apart: 7 -> 7, of which waited for: 6 -> 5; matrix products, arithmetic and copies ran while one was open for 13% -> 17% of each run, Pallas kernels for 0% -> 0%
where the time goes in v1:
time: 272 us; the launch traced here: 270 us
  waiting for transfers between devices  86.6 us (32%)
  local copies, waits for them, and re-layouts  77.2 us (28%)
  matrix products  32.7 us (12%)
  starting transfers between devices  29.4 us (11%)
  other arithmetic  28.8 us (11%)
  between operations  14.7 us (5%)
    all_to_all x1, waiting for transfers between devices, mamba_by_heads(): lax.all_to_all(jnp.stack([x_input, mixer_cot]), 'seq', split_axis=2, conc...  32 us
    reduce_scatter x1, waiting for transfers between devices, on_device(): lax.psum_scatter(jnp.concatenate(sums, axis=1), 'seq', scatter_dimension=...  26.3 us
    all_to_all x1, waiting for transfers between devices, mamba_by_heads(): back = lax.all_to_all(back, 'seq', split_axis=1, concat_axis=2, tiled=True)  24.8 us
    unnamed x91, local copies, waits for them, and re-layouts  18.8 us
    all_to_all x1, starting transfers between devices, mamba_by_heads(): lax.all_to_all(grad_decay, 'seq', split_axis=1, concat_axis=0, tiled=True)  13.7 us
    mul x16, local copies, waits for them, and re-layouts, advance(): return (fac[:, None, None] * carried + summ, carried)  10.9 us
    dynamic_update_slice x16, local copies, waits for them, and re-layouts, mixer_whole(): lax.scan(advance, jnp.zeros_like(summary[0]), (factor, summary))  9.87 us
    dot_general x3, matrix products, local_state(): jnp.einsum('hs,sn,shp->hnp', weights, b_float, inputs, precision=precise)  8.07 us
  transfers between devices with their start and end apart: 7, of which 5 were waited for; matrix products, arithmetic and copies ran while one was open for 17% of the time, Pallas kernels for 0%

profile of v1, /device:TPU:1, one launch (start us, length us, event | category | flops | bytes accessed | tf_op | source)
XLA Modules:
  0.0 270.0 jit_solution(10856526650221026137)
XLA Ops:
  11.6 1.3 constant_dynamic-update-slice_fusion.10
  12.9 1.2 constant_dynamic-update-slice_fusion.9
  14.1 1.2 constant_dynamic-update-slice_fusion.8
  15.4 1.2 constant_dynamic-update-slice_fusion.7
  17.9 1.2 constant_dynamic-update-slice_fusion.5
  20.4 1.3 constant_dynamic-update-slice_fusion.3
  21.6 6.4 %all-to-all-start.1 = ((f32[8,2,128]{2,1,0:T(2,128)}), f32[8,2,128]{2,1,0:T(2,128)S(1)}, u32[]{:S(2)}, u32[]{:S(2)}) async-start(f32[8,2,128]{2,1,0:T(2,128)} %constant_dynamic-update-slice_fusion.3), calls=%async_computation.1 | async-start | bytes 16384 | tf_op jit(solution)/shard_map/all_to_all | solution.py:116
  28.8 1.3 pad_maximum_fusion.1
  30.2 2.0 copy.341
  33.4 4.3 %all-to-all-start = ((bf16[2,128,2048]{1,0,2:T(2,128)(2,1)}), bf16[2,128,2048]{1,0,2:T(2,128)(2,1)S(1)}, u32[]{:S(2)}, u32[]{:S(2)}) async-start(bf16[2,128,2048]{1,0,2:T(2,128)(2,1)} %copy.341), calls=%async_computation | async-start | bytes 2097152 | tf_op jit(solution)/shard_map/all_to_all | solution.py:112
  43.3 32.0 %all-to-all-done = bf16[2,128,2048]{1,0,2:T(2,128)(2,1)S(1)} async-done(((bf16[2,128,2048]{1,0,2:T(2,128)(2,1)}), bf16[2,128,2048]{1,0,2:T(2,128)(2,1)S(1)}, u32[]{:S(2)}, u32[]{:S(2)}) %all-to-all-start) | async-done | bytes 1048608 | tf_op jit(solution)/shard_map/all_to_all | solution.py:112
  75.7 1.4 fusion.84
  78.7 2.3 fusion.35
  81.1 23.3 %while.88 = (s32[]{:T(128)}, f32[2,128,128]{2,1,0:T(8,128)S(1)}, f32[8,2,128,128]{3,2,1,0:T(8,128)S(1)}, f32[8,2,1,1]{1,3,2,0:T(1,128)}, f32[8,2]{1,0:T(8,128)},...) while((s32[]{:T(128)}, f32[2,128,128]{2,1,0:T(8,128)S(1)}, ...), condition=%wide.region_4.5_spmd.clone, body=%wide.region_3.4_spmd.clone.sunk | while | flops 131075 | bytes 656528 | solution.py:96
  104.4 1.3 copy.357
  105.7 2.9 %fusion.52 = (f32[8,128,2]{1,2,0:T(2,128)S(1)}, f32[8,128,256]{1,2,0}) fusion(bf16[8,128,2,128]{1,3,2,0:T(8,128)(2,1)S(1)} %bitcast.298, bf16[8,128,128]{2,1,0:T(8,128)(2,1)S(1)} %bitcast.309, f32[8,128,256]{1,2,0:T(8,128)} %bitcast.321), kind=kOutput, calls=%fused_computation.87 | convolution fusion | flops 403437568 | bytes 2891776
  108.6 1.6 fusion.59
  110.2 2.7 fusion.51
  112.9 1.6 convolution_bitcast_fusion.1
  114.6 14.9 %while.89 = (s32[]{:T(128)}, f32[2,128,128]{2,1,0:T(8,128)S(1)}, f32[8,2]{1,0:T(8,128)S(1)}, f32[8,2,128,128]{3,2,1,0:T(8,128)S(1)}, f32[8,2,128,128]{2,3,1,0:T(...) while((s32[]{:T(128)}, f32[2,128,128]{2,1,0:T(8,128)S(1)}, ...), condition=%wide.region_7.8_spmd.clone, body=%wide.region_5.7_spmd.clone.sunk | while | flops 196610 | bytes 1310920 | solution.py:96
  129.6 1.3 fusion.83
  130.9 1.8 while.85
  131.0 1.7 conditional.9
  133.6 3.3 %while.86 = (s32[]{:T(128)}, f32[128,2,4,128]{0,3,2,1:T(8,128)}, s32[]{:T(128)}, bf16[1024,256]{0,1:T(8,128)(2,1)S(1)}, s32[4]{0:T(128)S(1)}, /*index=5*/s32[128...) while((s32[]{:T(128)}, f32[128,2,4,128]{0,3,2,1:T(8,128)}, ...), condition=%wide.region_22.23_spmd.clone, body=%wide.region_17.22_spmd.clone.sunk | while | flops 271390848 | bytes 3031901 | solution.py:276
  133.6 3.3 %conditional.10 = (f32[128,2,4,128]{0,3,2,1:T(8,128)}) conditional(s32[]{:T(128)} %convert_element_type.165, f32[128,2,4,128]{0,3,2,1:T(8,128)} %get-tuple-element.1807, (s32[]{:T(128)}, bf16[1024,256]{0,1:T(8,128)(2,1)S(1)}, s32[]{:T(128)}, s32[4]{0:T(128)S(1)}, s32[128]{0:T(128)S(1)}, /*index=5*/bf16[1024,256]{0,1:T(8,128)(2,1)S(1)}, ...), branch_computations={%region_18.18_spmd, %region_19.21_spmd} | conditional | flops 271390848 | bytes 3031158 | solution.py:242
  134.1 2.8 %fusion.13 = f32[128,2,4,128]{0,3,2,1:T(8,128)} fusion(f32[128,2,4,128]{0,3,2,1:T(8,128)} %get-tuple-element.792, bf16[512,2,128,1]{0,2,3,1:T(8,128)(2,1)S(1)} %bitcast.313, bf16[512,2,128,1]{0,2,3,1:T(8,128)(2,1)S(1)} %bitcast.312, bf16[128,2,4,128]{3,0,2,1:T(8,128)(2,1)S(1)} %get-tuple-element.799, f32[2,4,128]{2,1,0:T(4,128)S(1)} %get-tuple-element.800, ...), kind=kOutput, calls=%fused_computation.19 | convolution fusion | flops 271187968 | bytes 1904640 | tf_op jit(solution)/shard_map/while/body/eval_jaxpr/cond/branch_1_fun/grtk,kgd->tgrd/dot_general | solution.py:272
  136.9 3.5 %fusion.53 = (f32[8,128,128]{1,2,0:T(8,128)}, f32[8,2,128,128]{3,2,1,0:T(8,128)}) fusion(f32[8,128,2]{1,2,0:T(2,128)S(1)} %copy.353, f32[8,2,128,128]{3,2,1,0:T(8,128)S(1)} %get-tuple-element.864, bf16[8,128,2,128]{1,3,2,0:T(8,128)(2,1)} %bitcast.316), kind=kOutput, calls=%fused_computation.91 | convolution fusion | flops 403046400 | bytes 3153920 | tf_op jit(solution)/shard_map/transpose(jvp(vmap(hs,sn,shp->hnp)))/dot_general | solution.py:50
  140.4 2.1 copy.423
  142.5 2.4 convolution_add_fusion
  145.0 1.4 convolution_add_fusion.1
  146.4 1.8 fusion.60
  150.5 4.2 %while.87 = (s32[]{:T(128)}, f32[128,2,4,128]{0,3,2,1:T(8,128)S(1)}, f32[1024,256]{0,1:T(8,128)}, f32[1024,256]{0,1:T(8,128)}, s32[]{:T(128)}, /*index=5*/bf16[1...) while((s32[]{:T(128)}, ...), condition=%wide.region_28.29_spmd.clone, body=%wide.region_23.28_spmd.clone.sunk | while | flops 675616896 | bytes 16667605 | solution.py:314
  150.5 4.2 %conditional.11 = ((f32[128,2,4,128]{0,3,2,1:T(8,128)S(1)}, f32[1024,256]{0,1:T(8,128)}, f32[1024,256]{0,1:T(8,128)})) conditional(s32[]{:T(128)} %convert_element_type.166, (f32[128,2,4,128]{0,3,2,1:T(8,128)S(1)}, f32[1024,256]{0,1:T(8,128)}, f32[1024,256]{0,1:T(8,128)}) %tuple.226, (s32[]{:T(128)}, bf16[1024,256]{0,1:T(8,128)(2,1)S(1)}, ...), branch_computations={%region_24.24_spmd, %region_25.27_spmd} | conditional | flops 675616896 | bytes 16666774 | solution.py:242
  154.7 1.6 copy.377
  156.3 2.6 copy.376
  158.9 3.3 %pad_maximum_fusion = f32[1024,768]{1,0:T(8,128)} fusion(f32[1024,128]{1,0:T(8,128)S(1)} %bitcast.322, f32[1024,128]{1,0:T(8,128)} %bitcast.323, f32[1024,256]{1,0:T(8,128)S(1)} %copy.377, f32[1024,256]{1,0:T(8,128)} %copy.376), kind=kLoop, calls=%fused_computation.65 | loop fusion | flops 2359296 | bytes 6291456 | tf_op jit(solution)/shard_map/concatenate | solution.py:322
  164.1 2.1 fusion.43
  166.2 2.3 fusion.47
  169.2 3.0 %fusion.46 = bf16[8,128,2,128]{1,3,2,0:T(8,128)(2,1)S(1)} fusion(bf16[8,128,2,128]{1,3,2,0:T(8,128)(2,1)S(1)} %bitcast.317, f32[8,128,2,128]{1,3,2,0:T(8,128)} %bitcast.329, f32[2]{0:T(128)S(1)} %dynamic_slice.54, f32[8,128,2]{1,2,0:T(2,128)S(1)} %copy.352, f32[8,128,128]{2,1,0:T(8,128)} %fusion.90, f32[8,2,128]{2,1,0:T(2,128)S(1)} %copy-done.31, ...), kind=kOutput, calls=%fused_computation.81 | convolution fusion | flops 405012480 | bytes 2768904 | tf_op jit(solution)/shard_map/jvp(vmap(hts,shp->thp))/dot_general | solution.py:64
  174.1 2.5 reduce_window_sum.46
  176.7 2.5 reduce_window_sum.47
  179.8 13.7 %all-to-all-start.3 = ((f32[2,8,128]{2,0,1:T(2,128)}), f32[2,8,128]{2,0,1:T(2,128)S(1)}, u32[]{:S(2)}, u32[]{:S(2)}) async-start(f32[2,8,128]{2,0,1:T(2,128)} %copy.384), calls=%async_computation.4 | async-start | bytes 16384 | tf_op jit(solution)/shard_map/all_to_all | solution.py:138
  194.7 2.1 copy.362
  196.7 2.2 all-to-all-done.3
  199.0 3.6 %all-to-all-start.2 = ((bf16[2,1024,256]{2,0,1:T(2,128)(2,1)}), bf16[2,1024,256]{2,0,1:T(2,128)(2,1)S(1)}, u32[]{:S(2)}, u32[]{:S(2)}) async-start(bf16[2,1024,256]{2,0,1:T(2,128)(2,1)} %copy.362), calls=%async_computation.2 | async-start | bytes 2097152 | tf_op jit(solution)/shard_map/all_to_all | solution.py:137
  204.3 24.8 %all-to-all-done.2 = bf16[2,1024,256]{2,0,1:T(2,128)(2,1)S(1)} async-done(((bf16[2,1024,256]{2,0,1:T(2,128)(2,1)}), bf16[2,1024,256]{2,0,1:T(2,128)(2,1)S(1)}, u32[]{:S(2)}, u32[]{:S(2)}) %all-to-all-start.2) | async-done | bytes 1048608 | tf_op jit(solution)/shard_map/all_to_all | solution.py:137
  229.3 26.3 %reduce-scatter.2.cloned.1.call-done = f32[128,768]{1,0:T(8,128)} async-done(((f32[1024,768]{1,0:T(8,128)}), f32[128,768]{1,0:T(8,128)}) %reduce-scatter.2.cloned.1.call-update) | async-done | bytes 393232 | tf_op jit(solution)/shard_map/reduce_scatter | solution.py:321
  256.5 1.4 collective-permute-start
  (278 shorter events, 78.2 us)
Async XLA Ops:
  7.2 68.6 %all-gather.2.cloned.1.call-start = ((), (), s32[]{:S(2)}) async-start(), calls=%async_computation.5 | async-start | bytes 1769472 | tf_op jit(solution)/shard_map/all_gather | solution.py:201
  21.6 11.8 %all-to-all-start.1 = ((f32[8,2,128]{2,1,0:T(2,128)}), f32[8,2,128]{2,1,0:T(2,128)S(1)}, u32[]{:S(2)}, u32[]{:S(2)}) async-start(f32[8,2,128]{2,1,0:T(2,128)} %constant_dynamic-update-slice_fusion.3), calls=%async_computation.1 | async-start | bytes 16384 | tf_op jit(solution)/shard_map/all_to_all | solution.py:116
  30.2 7.6 %copy-start.20 = (bf16[128,1024]{1,0:T(8,128)(2,1)S(1)}, bf16[128,1024]{1,0:T(8,128)(2,1)}, u32[]{:S(2)}) copy-start(bf16[128,1024]{1,0:T(8,128)(2,1)} %param.37) | copy-start | bytes 786436
  30.2 7.7 %copy-start.21 = (bf16[128,1024]{1,0:T(8,128)(2,1)S(1)}, bf16[128,1024]{1,0:T(8,128)(2,1)}, u32[]{:S(2)}) copy-start(bf16[128,1024]{1,0:T(8,128)(2,1)} %param.33) | copy-start | bytes 786436
  33.4 42.0 %all-to-all-start = ((bf16[2,128,2048]{1,0,2:T(2,128)(2,1)}), bf16[2,128,2048]{1,0,2:T(2,128)(2,1)S(1)}, u32[]{:S(2)}, u32[]{:S(2)}) async-start(bf16[2,128,2048]{1,0,2:T(2,128)(2,1)} %copy.341), calls=%async_computation | async-start | bytes 2097152 | tf_op jit(solution)/shard_map/all_to_all | solution.py:112
  37.7 217.9 %reduce-scatter.2.cloned.1.call-start = ((), (), s32[]{:S(2)}) async-start(), calls=%async_computation.6 | async-start | bytes 3538944 | tf_op jit(solution)/shard_map/reduce_scatter | solution.py:321
  39.6 35.9 %copy-start.32 = (f32[8]{0:T(128)}, f32[8]{0:T(128)S(1)}, u32[]{:S(2)}) copy-start(f32[8]{0:T(128)S(1)} %convert_reduce_fusion.4) | copy-start | bytes 100
  41.0 34.6 %copy-start.25 = (f32[8,128]{1,0:T(8,128)}, f32[8,128]{1,0:T(8,128)S(1)}, u32[]{:S(2)}) copy-start(f32[8,128]{1,0:T(8,128)S(1)} %get-tuple-element.1394) | copy-start | bytes 12292
  41.2 67.4 %copy-start.22 = (pred[8,128,128]{2,1,0:T(8,128)(4,1)}, pred[8,128,128]{2,1,0:T(8,128)(4,1)S(1)}, u32[]{:S(2)}) copy-start(pred[8,128,128]{2,1,0:T(8,128)(4,1)S(1)} %compare_and_fusion.3) | copy-start | bytes 393220
  42.6 33.0 %copy-start.28 = (f32[8,2]{0,1:T(2,128)}, f32[8,2]{0,1:T(2,128)S(1)}, u32[]{:S(2)}) copy-start(f32[8,2]{0,1:T(2,128)S(1)} %slice_reduce_fusion) | copy-start | bytes 196
  75.7 32.9 %copy-start.10 = (bf16[1,8,128,256]{2,3,1,0:T(8,128)(2,1)}, bf16[1,8,128,256]{2,3,1,0:T(8,128)(2,1)S(1)}, u32[]{:S(2)}) copy-start(bf16[1,8,128,256]{2,3,1,0:T(8,128)(2,1)S(1)} %get-tuple-element.1386) | copy-start | bytes 1572868
  75.7 37.2 %copy-start.1 = (bf16[1,8,128,256]{2,3,1,0:T(8,128)(2,1)}, bf16[1,8,128,256]{2,3,1,0:T(8,128)(2,1)S(1)}, u32[]{:S(2)}) copy-start(bf16[1,8,128,256]{2,3,1,0:T(8,128)(2,1)S(1)} %get-tuple-element.1387) | copy-start | bytes 1572868
  77.3 35.5 %copy-start.6 = (bf16[1024,128]{1,0:T(8,128)(2,1)}, bf16[1024,128]{1,0:T(8,128)(2,1)S(1)}, u32[]{:S(2)}) copy-start(bf16[1024,128]{1,0:T(8,128)(2,1)S(1)} %copy.350) | copy-start | bytes 786436
  77.5 3.5 %copy-start.3 = (bf16[1024,128]{1,0:T(8,128)(2,1)}, bf16[1024,128]{1,0:T(8,128)(2,1)S(1)}, u32[]{:S(2)}) copy-start(bf16[1024,128]{1,0:T(8,128)(2,1)S(1)} %copy.351) | copy-start | bytes 786436
  77.6 1.1 copy-start.8
  104.4 4.3 %copy-start.30 = (f32[8,2,128]{2,1,0:T(2,128)S(1)}, f32[8,2,128]{2,1,0:T(2,128)}, u32[]{:S(2)}) copy-start(f32[8,2,128]{2,1,0:T(2,128)} %copy.344) | copy-start | bytes 24580
  105.7 3.0 %copy-start.19 = (f32[8,128,128]{2,1,0:T(8,128)S(1)}, f32[8,128,128]{2,1,0:T(8,128)}, u32[]{:S(2)}) copy-start(f32[8,128,128]{2,1,0:T(8,128)} %fusion.90) | copy-start | bytes 1572868
  108.6 1.6 copy-start.27
  129.5 1.4 copy-start
  129.5 1.4 copy-start.24
  129.6 1.4 copy-start.34
  136.9 5.6 %copy-start.4 = (bf16[1024,128]{1,0:T(8,128)(2,1)S(1)}, bf16[1024,128]{1,0:T(8,128)(2,1)}, u32[]{:S(2)}) copy-start(bf16[1024,128]{1,0:T(8,128)(2,1)} %copy-done.3) | copy-start | bytes 786436
  140.4 4.6 %copy-start.7 = (bf16[1024,128]{1,0:T(8,128)(2,1)S(1)}, bf16[1024,128]{1,0:T(8,128)(2,1)}, u32[]{:S(2)}) copy-start(bf16[1024,128]{1,0:T(8,128)(2,1)} %copy-done.6) | copy-start | bytes 786436
  142.5 2.5 copy-start.13
  142.5 2.5 copy-start.16
  154.7 4.2 %copy-start.14 = (f32[8,128,128]{2,1,0:T(8,128)S(1)}, f32[8,128,128]{2,1,0:T(8,128)}, u32[]{:S(2)}) copy-start(f32[8,128,128]{2,1,0:T(8,128)} %convolution_add_fusion) | copy-start | bytes 1572868
  162.2 0.7 copy-start.35
  162.2 1.0 copy-start.5
  162.2 1.9 copy-start.2
  162.2 1.9 copy-start.23
  162.2 1.9 copy-start.31
  162.2 4.0 %copy-start.9 = (f32[8,128,128]{2,1,0:T(8,128)S(1)}, f32[8,128,128]{2,1,0:T(8,128)}, u32[]{:S(2)}) copy-start(f32[8,128,128]{2,1,0:T(8,128)} %copy-done.8) | copy-start | bytes 1572868
  166.2 2.9 %copy-start.11 = (bf16[1,8,128,256]{2,3,1,0:T(8,128)(2,1)S(1)}, bf16[1,8,128,256]{2,3,1,0:T(8,128)(2,1)}, u32[]{:S(2)}) copy-start(bf16[1,8,128,256]{2,3,1,0:T(8,128)(2,1)} %copy-done.10) | copy-start | bytes 1572868
  169.1 4.5 %copy-start.29 = (f32[8,2]{0,1:T(2,128)S(1)}, f32[8,2]{0,1:T(2,128)}, u32[]{:S(2)}) copy-start(f32[8,2]{0,1:T(2,128)} %copy-done.28) | copy-start | bytes 196
  169.1 4.5 %copy-start.33 = (f32[8]{0:T(128)S(1)}, f32[8]{0:T(128)}, u32[]{:S(2)}) copy-start(f32[8]{0:T(128)} %copy-done.32) | copy-start | bytes 100
  169.1 4.6 %copy-start.12 = (f32[8,2,128,128]{3,2,1,0:T(8,128)S(1)}, f32[8,2,128,128]{3,2,1,0:T(8,128)}, u32[]{:S(2)}) copy-start(f32[8,2,128,128]{3,2,1,0:T(8,128)} %get-tuple-element.1401) | copy-start | bytes 3145732
  169.2 4.6 %copy-start.15 = (f32[8,128,128]{1,2,0:T(8,128)S(1)}, f32[8,128,128]{1,2,0:T(8,128)}, u32[]{:S(2)}) copy-start(f32[8,128,128]{1,2,0:T(8,128)} %copy.446) | copy-start | bytes 1572868
  172.1 1.7 copy-start.26
  179.8 19.2 %all-to-all-start.3 = ((f32[2,8,128]{2,0,1:T(2,128)}), f32[2,8,128]{2,0,1:T(2,128)S(1)}, u32[]{:S(2)}, u32[]{:S(2)}) async-start(f32[2,8,128]{2,0,1:T(2,128)} %copy.384), calls=%async_computation.4 | async-start | bytes 16384 | tf_op jit(solution)/shard_map/all_to_all | solution.py:138
  194.7 7.9 %copy-start.17 = (bf16[128,2,4,128]{0,3,2,1:T(8,128)(2,1)S(1)}, bf16[128,2,4,128]{0,3,2,1:T(8,128)(2,1)}, u32[]{:S(2)}) copy-start(bf16[128,2,4,128]{0,3,2,1:T(8,128)(2,1)} %get-tuple-element.1371) | copy-start | bytes 786436
  199.0 30.2 %all-to-all-start.2 = ((bf16[2,1024,256]{2,0,1:T(2,128)(2,1)}), bf16[2,1024,256]{2,0,1:T(2,128)(2,1)S(1)}, u32[]{:S(2)}, u32[]{:S(2)}) async-start(bf16[2,1024,256]{2,0,1:T(2,128)(2,1)} %copy.362), calls=%async_computation.2 | async-start | bytes 2097152 | tf_op jit(solution)/shard_map/all_to_all | solution.py:137
  256.5 4.7 %collective-permute-start = (f32[128,256]{1,0:T(8,128)S(1)}, f32[128,256]{1,0:T(8,128)S(1)}, u32[]{:S(2)}, u32[]{:S(2)}) collective-permute-start(f32[128,256]{1,0:T(8,128)S(1)} %slice.80), channel_id=1, source_target_pairs={{0,1},{1,0},{2,3},{3,2},{4,5},{5,4},{6,7},{7,6},{8,9},{9,8},{10,11... | collective-permute-start | bytes 393224 | tf_op jit(solution)/shard_map/ppermute | solution.py:329
  258.0 2.6 copy-start.18
Sparse Core Ops, SparseCore 0:
  11.7 63.4 all-gather.1
  162.3 93.2 reduce-scatter.1
